TPU v7x, 256 devices: a whole 4x4x8 slice. The times are simulated.
256 devices in a mesh: gx: 32 (over z_lo, y, core), gy: 4 (over x), gz: 2 (over z_hi).
Axes of the slice: x: 4, y: 4, z: 8 (z_hi: 2, z_lo: 4; z = z_hi * 4 + z_lo), core: 2. Of those that a mesh axis runs over, the one named last changes fastest.
Arguments:
- f_pop: float32 [19, 128, 64, 256], P(None, 'gx', 'gy', 'gz'), may hold values from 0.02 to 0.1
- g_pop: float32 [19, 128, 64, 256], P(None, 'gx', 'gy', 'gz'), may hold values from -0.2 to 0.2
- displacement: int32 [1], replicated, may hold values from 33 to 47
Outputs:
- f_new: float32 [19, 128, 64, 256], P(None, 'gx', 'gy', 'gz')
- g_new: float32 [19, 128, 64, 256], P(None, 'gx', 'gy', 'gz')
All inputs are finite; a program needn't handle non-finite values.
Results may differ from a plain program's by a relative error of at most 0.0001.
Values sent between devices are 32-bit elements; how exact they have to be, the bound alone decides.
No kernel may reach another device: no remote copies, remote signals or barrier semaphores. Data moves between devices by JAX's collectives and lax.ppermute only.
A program may use at most 64 MiB of HBM per device.

v0:
```python
import jax
import jax.numpy as jnp
from jax import lax
from jax.sharding import PartitionSpec as P

VELOCITIES = [
    (0, 0, 0),
    (1, 0, 0),
    (1, 1, 0),
    (1, -1, 0),
    (1, 0, 1),
    (1, 0, -1),
    (-1, 0, 0),
    (-1, -1, 0),
    (-1, 1, 0),
    (-1, 0, -1),
    (-1, 0, 1),
    (0, 1, 0),
    (0, -1, 0),
    (0, 0, 1),
    (0, 0, -1),
    (0, 1, 1),
    (0, -1, -1),
    (0, 1, -1),
    (0, -1, 1),
]
BULK_COEF = 0.5
STIFFNESS = 0.5
TAU_FLUID = 0.8
TAU_ORDER = 0.9


def with_halo(cells, sides, width):
    for axis, dim in sides:
        count = lax.axis_size(axis)
        head = lax.slice_in_dim(cells, 0, width, axis=dim)
        tail = lax.slice_in_dim(cells, cells.shape[dim] - width, cells.shape[dim], axis=dim)
        cells = jnp.concatenate(
            [
                lax.ppermute(tail, axis, [(i, (i + 1) % count) for i in range(count)]),
                cells,
                lax.ppermute(head, axis, [((i + 1) % count, i) for i in range(count)]),
            ],
            axis=dim,
        )
    return cells


def lattice_weight(number):
    steps_sq = sum((abs(comp) for comp in VELOCITIES[number]))
    if steps_sq == 0:
        return 1.0 / 3.0
    if steps_sq == 1:
        return 1.0 / 18.0
    return 1.0 / 36.0


def along(number, values, base):
    result = jnp.zeros_like(base)
    for axis_id in range(3):
        comp = VELOCITIES[number][axis_id]
        if comp != 0:
            result = result + comp * values[axis_id]
    return result


def collide(f_pop, g_pop, order_field, laplace, slopes):
    density = jnp.sum(f_pop, axis=0)
    chemical = (
        BULK_COEF * (order_field * order_field * order_field - order_field) - STIFFNESS * laplace
    )
    forces = [chemical * slope for slope in slopes]
    moments = []
    for axis_id in range(3):
        moment = jnp.zeros_like(density)
        for number in range(19):
            comp = VELOCITIES[number][axis_id]
            if comp != 0:
                moment = moment + comp * f_pop[number]
        moments.append(moment)
    flows = [(moments[axis_id] + 0.5 * forces[axis_id]) / density for axis_id in range(3)]
    speed_sq = flows[0] * flows[0] + flows[1] * flows[1] + flows[2] * flows[2]
    flow_force = flows[0] * forces[0] + flows[1] * forces[1] + flows[2] * forces[2]
    f_posts = []
    g_eqs = []
    for number in range(19):
        weight = lattice_weight(number)
        proj_flow = along(number, flows, density)
        proj_force = along(number, forces, density)
        shape_term = 3.0 * proj_flow + 4.5 * proj_flow * proj_flow - 1.5 * speed_sq
        f_eq = weight * density * (1.0 + shape_term)
        source = (
            (1.0 - 0.5 / TAU_FLUID)
            * weight
            * (3.0 * (proj_force - flow_force) + 9.0 * proj_flow * proj_force)
        )
        f_posts.append(f_pop[number] - (f_pop[number] - f_eq) / TAU_FLUID + source)
        g_eqs.append(weight * (3.0 * chemical + order_field * shape_term))
    rest_eq = order_field
    for number in range(1, 19):
        rest_eq = rest_eq - g_eqs[number]
    g_eqs[0] = rest_eq
    g_posts = [g_pop[number] - (g_pop[number] - g_eqs[number]) / TAU_ORDER for number in range(19)]
    return (jnp.stack(f_posts), jnp.stack(g_posts))


def window(whole, begin, rows, whole_rows):
    begin = jnp.mod(begin, whole_rows)
    doubled = jnp.concatenate([whole, whole], axis=1)
    return lax.dynamic_slice_in_dim(doubled, begin, rows, 1)


def sliding(edges, shift):
    extended = with_halo(edges, (("gx", 1),), 1)
    below = extended[:, 0]
    above = extended[:, 3]
    whole_below, whole_above = (
        lax.all_gather(below, "gy", axis=1, tiled=True),
        lax.all_gather(above, "gy", axis=1, tiled=True),
    )
    rows = below.shape[1]
    whole_rows = whole_below.shape[1]
    start = lax.axis_index("gy") * rows
    return (
        window(whole_below, start - shift, rows, whole_rows),
        window(whole_above, start + shift, rows, whole_rows),
    )


def extend_x(posts, below, above):
    rows, layers = (posts.shape[2], posts.shape[3])
    lower = jnp.concatenate(
        [
            jnp.zeros((1, rows, layers), jnp.float32),
            below,
            jnp.zeros((13, rows, layers), jnp.float32),
        ],
        axis=0,
    )
    upper = jnp.concatenate(
        [
            jnp.zeros((6, rows, layers), jnp.float32),
            above,
            jnp.zeros((8, rows, layers), jnp.float32),
        ],
        axis=0,
    )
    return jnp.concatenate([lower[:, None], posts, upper[:, None]], axis=1)


def local(f_pop, g_pop, displacement):
    shift = displacement[0]
    width_x, width_y, width_z = (f_pop.shape[1], f_pop.shape[2], f_pop.shape[3])
    order_field = jnp.sum(g_pop, axis=0)
    phase_edges = jnp.stack([order_field[0], order_field[-1]])[None]
    phase_below, phase_above = sliding(phase_edges, shift)
    neigh_xm = jnp.concatenate([phase_below, order_field[:-1]], axis=0)
    neigh_xp = jnp.concatenate([order_field[1:], phase_above], axis=0)
    padded = with_halo(order_field, (("gy", 1), ("gz", 2)), 1)
    neigh_ym = padded[:, :-2, 1:-1]
    neigh_yp = padded[:, 2:, 1:-1]
    neigh_zm = padded[:, 1:-1, :-2]
    neigh_zp = padded[:, 1:-1, 2:]
    laplace = neigh_xm + neigh_xp + neigh_ym + neigh_yp + neigh_zm + neigh_zp - 6.0 * order_field
    slopes = [0.5 * (neigh_xp - neigh_xm), 0.5 * (neigh_yp - neigh_ym), 0.5 * (neigh_zp - neigh_zm)]
    f_post, g_post = collide(f_pop, g_pop, order_field, laplace, slopes)
    pop_edges = jnp.concatenate(
        [
            jnp.stack([f_post[6:11, 0], f_post[1:6, -1]], axis=1),
            jnp.stack([g_post[6:11, 0], g_post[1:6, -1]], axis=1),
        ],
        axis=0,
    )
    pop_below, pop_above = sliding(pop_edges, shift)
    layered = jnp.concatenate(
        [
            extend_x(f_post, pop_below[0:5], pop_above[0:5]),
            extend_x(g_post, pop_below[5:10], pop_above[5:10]),
        ],
        axis=0,
    )
    results = []
    padded_all = with_halo(layered, (("gy", 2), ("gz", 3)), 1)
    for number in range(38):
        vel_x, vel_y, vel_z = VELOCITIES[number % 19]
        results.append(
            padded_all[
                number,
                1 - vel_x : 1 - vel_x + width_x,
                1 - vel_y : 1 - vel_y + width_y,
                1 - vel_z : 1 - vel_z + width_z,
            ]
        )
    f_new = jnp.stack(results[:19])
    g_new = jnp.stack(results[19:])
    return (f_new, g_new)


def solution(mesh):
    return jax.shard_map(
        local,
        mesh=mesh,
        in_specs=(P(None, "gx", "gy", "gz"), P(None, "gx", "gy", "gz"), P()),
        out_specs=(P(None, "gx", "gy", "gz"), P(None, "gx", "gy", "gz")),
        check_vma=False,
    )
```

profile of v0, /device:TPU:6, one launch (start us, length us, event | category | flops | bytes accessed | tf_op | source)
XLA Modules:
  0.0 120.2 jit_solution(16818710644719364818)
XLA Ops:
  0.7 1.2 %reduce_sum.19 = f32[4,16,128]{2,1,0:T(8,128)S(1)} reduce(f32[19,4,16,128]{3,2,1,0:T(8,128)} %param.4, f32[]{:T(128)} %constant.95.clone.1), dimensions={0}, to_apply=%region_1.2 | reduce | flops 147456 | bytes 655364 | tf_op jit(solution)/shard_map/reduce_sum | solution.py:154
  1.9 0.9 collective-permute-start.3
  2.8 2.4 %collective-permute-start.2 = (f32[4,1,128]{2,1,0:T(1,128)S(1)}, f32[4,1,128]{2,1,0:T(1,128)S(1)}, u32[]{:S(2)}, u32[]{:S(2)}) collective-permute-start(f32[4,1,128]{2,1,0:T(1,128)S(1)} %get-tuple-element.109), channel_id=1, source_target_pairs={{0,2},{2,4},{4,6},{6,0},{1,3},{3,5},{5,7},{7,1},{8,10},{10,12},{12... | collective-permute-start | bytes 6152 | tf_op jit(solution)/shard_map/ppermute | solution.py:40
  5.2 6.0 %collective-permute-start.1 = (f32[1,1,16,128]{3,2,1,0:T(8,128)S(1)}, f32[1,1,16,128]{3,2,1,0:T(8,128)S(1)}, u32[]{:S(2)}, u32[]{:S(2)}) collective-permute-start(f32[1,1,16,128]{3,2,1,0:T(8,128)S(1)} %get-tuple-element.114), channel_id=1, source_target_pairs={{8,0},{16,8},{24,16},{32,24},{40,32},{48,40},{56,48},{64,56},{72,6... | collective-permute-start | bytes 24584 | tf_op jit(solution)/shard_map/ppermute | solution.py:42
  12.0 0.1 pad.67.clone
  12.1 0.1 pad.60.clone
  12.1 1.1 reduce_sum.18
  13.3 0.1 fusion.109
  13.4 4.5 %collective-permute-start.5 = (f32[4,18,1]{2,1,0:T(8,128)S(1)}, f32[4,18,1]{2,1,0:T(8,128)S(1)}, u32[]{:S(2)}, u32[]{:S(2)}) collective-permute-start(f32[4,18,1]{2,1,0:T(8,128)S(1)} %get-tuple-element.106), channel_id=1, source_target_pairs={{1,0},{0,1},{3,2},{2,3},{5,4},{4,5},{7,6},{6,7},{9,8},{8,9},{11,10... | collective-permute-start | bytes 872 | tf_op jit(solution)/shard_map/ppermute | solution.py:42
  17.9 1.4 %collective-permute-start.4 = (f32[4,18,1]{2,1,0:T(8,128)S(1)}, f32[4,18,1]{2,1,0:T(8,128)S(1)}, u32[]{:S(2)}, u32[]{:S(2)}) collective-permute-start(f32[4,18,1]{2,1,0:T(8,128)S(1)} %get-tuple-element.107), channel_id=1, source_target_pairs={{0,1},{1,0},{2,3},{3,2},{4,5},{5,4},{6,7},{7,6},{8,9},{9,8},{10,11... | collective-permute-start | bytes 872 | tf_op jit(solution)/shard_map/ppermute | solution.py:40
  19.4 11.9 %all-gather = f32[1,1,64,128]{3,2,1,0:T(8,128)S(1)} all-gather(f32[1,1,16,128]{3,2,1,0:T(8,128)S(1)} %collective-permute-done), channel_id=2, replica_groups=mesh['gx'=32,'gy'=4,'gz'=2] {'gy'}, dimensions={2}, use_global_device_ids=true | all-gather | bytes 40960 | tf_op jit(solution)/shard_map/all_gather | solution.py:118
  31.3 11.9 %all-gather.1 = f32[1,1,64,128]{3,2,1,0:T(8,128)S(1)} all-gather(f32[1,1,16,128]{3,2,1,0:T(8,128)S(1)} %collective-permute-done.1), channel_id=3, replica_groups=mesh['gx'=32,'gy'=4,'gz'=2] {'gy'}, dimensions={2}, use_global_device_ids=true | all-gather | bytes 40960 | tf_op jit(solution)/shard_map/all_gather | solution.py:119
  43.2 1.4 %bitcast_subtract_fusion.16 = (f32[4,16,128]{2,1,0:T(8,128)S(1)}, f32[4,16,128]{2,1,0:T(8,128)S(1)}, f32[4,16,128]{2,1,0:T(8,128)S(1)}, f32[4,16,128]{2,1,0:T(8,...) fusion(f32[4,16,128]{2,1,0:T(8,128)S(1)} %reduce_sum.19, ...), kind=kLoop, calls=%fused_computation.190 | loop fusion | flops 2064384 | bytes 1512000 | tf_op jit(solution)/shard_map/sub | solution.py:103
  45.4 0.1 collective-permute-start.7
  45.5 0.5 collective-permute-start.6
  46.0 0.8 copy.371
  47.3 6.0 %collective-permute-done.6 = f32[10,1,16,128]{3,2,1,0:T(8,128)S(1)} collective-permute-done((f32[10,1,16,128]{3,2,1,0:T(8,128)S(1)}, f32[10,1,16,128]{3,2,1,0:T(8,128)S(1)}, u32[]{:S(2)}, u32[]{:S(2)}) %collective-permute-start.6) | collective-permute-done | bytes 81952 | tf_op jit(solution)/shard_map/ppermute | solution.py:40
  53.3 0.1 copy.282
  53.4 12.4 %all-gather.2 = f32[10,1,64,128]{3,1,0,2:T(1,128)S(1)} all-gather(f32[10,1,16,128]{3,1,0,2:T(1,128)S(1)} %copy.282), channel_id=4, replica_groups=mesh['gx'=32,'gy'=4,'gz'=2] {'gy'}, dimensions={2}, use_global_device_ids=true | all-gather | bytes 409600 | tf_op jit(solution)/shard_map/all_gather | solution.py:118
  65.9 0.1 copy.284
  66.0 12.4 %all-gather.3 = f32[10,1,64,128]{3,1,0,2:T(1,128)S(1)} all-gather(f32[10,1,16,128]{3,1,0,2:T(1,128)S(1)} %copy.284), channel_id=5, replica_groups=mesh['gx'=32,'gy'=4,'gz'=2] {'gy'}, dimensions={2}, use_global_device_ids=true | all-gather | bytes 409600 | tf_op jit(solution)/shard_map/all_gather | solution.py:119
  78.5 0.1 maximum_bitcast_fusion.2
  78.6 0.1 maximum_bitcast_fusion.1
  78.7 0.2 fusion
  78.9 0.7 collective-permute-start.8
  79.6 1.7 %collective-permute-start.9 = (f32[38,6,1,128]{3,0,2,1:T(8,128)S(1)}, f32[38,6,1,128]{3,0,2,1:T(8,128)S(1)}, u32[]{:S(2)}, u32[]{:S(2)}) collective-permute-start(f32[38,6,1,128]{3,0,2,1:T(8,128)S(1)} %copy.290), channel_id=1, source_target_pairs={{2,0},{4,2},{6,4},{0,6},{3,1},{5,3},{7,5},{1,7},{10,8},{12,10},{14... | collective-permute-start | bytes 350216 | tf_op jit(solution)/shard_map/ppermute | solution.py:42
  81.3 2.6 %collective-permute-done.8 = f32[38,6,1,128]{3,0,2,1:T(8,128)S(1)} collective-permute-done((f32[38,6,1,128]{3,0,2,1:T(8,128)S(1)}, f32[38,6,1,128]{3,0,2,1:T(8,128)S(1)}, u32[]{:S(2)}, u32[]{:S(2)}) %collective-permute-start.8) | collective-permute-done | bytes 116768 | tf_op jit(solution)/shard_map/ppermute | solution.py:40
  83.8 0.1 copy.289
  84.0 1.9 %collective-permute-done.9 = f32[38,6,1,128]{3,0,2,1:T(8,128)S(1)} collective-permute-done((f32[38,6,1,128]{3,0,2,1:T(8,128)S(1)}, f32[38,6,1,128]{3,0,2,1:T(8,128)S(1)}, u32[]{:S(2)}, u32[]{:S(2)}) %collective-permute-start.9) | collective-permute-done | bytes 116768 | tf_op jit(solution)/shard_map/ppermute | solution.py:42
  85.9 0.1 copy.291
  86.0 0.5 pad_maximum_fusion
  86.5 3.2 %fusion.105 = (f32[38,6,18,1]{3,2,1,0:T(8,128)}, f32[38,6,18,1]{3,2,1,0:T(8,128)}) fusion(f32[38,6,18,128]{3,2,1,0:T(8,128)S(1)} %pad_maximum_fusion), kind=kLoop, calls=%fused_computation.399 | loop fusion | bytes 65664 | tf_op jit(solution)/shard_map/slice | solution.py:36
  89.7 3.0 %copy.294 = f32[38,6,18,1]{0,2,3,1:T(8,128)S(1)} copy(f32[38,6,18,1]{3,2,1,0:T(8,128)} %get-tuple-element.53) | data formatting | bytes 32832 | tf_op jit(solution)/shard_map/slice | solution.py:37
  92.8 4.6 %collective-permute-start.10 = (f32[38,6,18,1]{0,2,3,1:T(8,128)S(1)}, f32[38,6,18,1]{0,2,3,1:T(8,128)S(1)}, u32[]{:S(2)}, u32[]{:S(2)}) collective-permute-start(f32[38,6,18,1]{0,2,3,1:T(8,128)S(1)} %copy.294), channel_id=1, source_target_pairs={{0,1},{1,0},{2,3},{3,2},{4,5},{5,4},{6,7},{7,6},{8,9},{9,8},{10,11... | collective-permute-start | bytes 49256 | tf_op jit(solution)/shard_map/ppermute | solution.py:40
  97.4 3.0 %copy.296 = f32[38,6,18,1]{0,2,3,1:T(8,128)S(1)} copy(f32[38,6,18,1]{3,2,1,0:T(8,128)} %get-tuple-element.52) | data formatting | bytes 32832 | tf_op jit(solution)/shard_map/slice | solution.py:36
  100.4 1.5 %collective-permute-start.11 = (f32[38,6,18,1]{0,2,3,1:T(8,128)S(1)}, f32[38,6,18,1]{0,2,3,1:T(8,128)S(1)}, u32[]{:S(2)}, u32[]{:S(2)}) collective-permute-start(f32[38,6,18,1]{0,2,3,1:T(8,128)S(1)} %copy.296), channel_id=1, source_target_pairs={{1,0},{0,1},{3,2},{2,3},{5,4},{4,5},{7,6},{6,7},{9,8},{8,9},{11,10... | collective-permute-start | bytes 49256 | tf_op jit(solution)/shard_map/ppermute | solution.py:42
  101.9 2.8 %copy.295 = f32[38,6,18,1]{3,2,1,0:T(8,128)} copy(f32[38,6,18,1]{0,2,3,1:T(8,128)S(1)} %collective-permute-done.10) | data formatting | bytes 32832 | tf_op jit(solution)/shard_map/ppermute | solution.py:40
  104.7 0.9 constant_dynamic-update-slice_fusion.91
  105.5 3.2 %collective-permute-done.11 = f32[38,6,18,1]{0,2,3,1:T(8,128)S(1)} collective-permute-done((f32[38,6,18,1]{0,2,3,1:T(8,128)S(1)}, f32[38,6,18,1]{0,2,3,1:T(8,128)S(1)}, u32[]{:S(2)}, u32[]{:S(2)}) %collective-permute-start.11) | collective-permute-done | bytes 16448 | tf_op jit(solution)/shard_map/ppermute | solution.py:42
  108.7 2.8 %copy.297 = f32[38,6,18,1]{3,2,1,0:T(8,128)} copy(f32[38,6,18,1]{0,2,3,1:T(8,128)S(1)} %collective-permute-done.11) | data formatting | bytes 32832 | tf_op jit(solution)/shard_map/ppermute | solution.py:42
  111.5 0.9 constant_dynamic-update-slice_fusion.90
  112.5 1.7 %copy-done.1 = f32[38,6,18,1]{3,2,1,0:T(8,128)S(1)} copy-done((f32[38,6,18,1]{3,2,1,0:T(8,128)S(1)}, f32[38,6,18,1]{3,2,1,0:T(8,128)}, u32[]{:S(2)}) %copy-start.1) | copy-done | bytes 16440
  114.2 0.1 constant_dynamic-update-slice_fusion.86
  114.3 1.7 %copy-done = f32[38,6,18,1]{3,2,1,0:T(8,128)S(1)} copy-done((f32[38,6,18,1]{3,2,1,0:T(8,128)S(1)}, f32[38,6,18,1]{3,2,1,0:T(8,128)}, u32[]{:S(2)}) %copy-start) | copy-done | bytes 16440
  116.0 0.1 constant_dynamic-update-slice_fusion.85
  116.1 0.1 constant_dynamic-update-slice_fusion.82
  116.2 0.1 constant_dynamic-update-slice_fusion.81
  116.3 1.0 copy-done.5
  117.3 0.1 constant_dynamic-update-slice_fusion.80
  117.4 0.1 constant_dynamic-update-slice_fusion.79
  117.5 0.1 constant_dynamic-update-slice_fusion.72
  117.6 0.1 constant_dynamic-update-slice_fusion.71
  117.7 0.1 constant_dynamic-update-slice_fusion.78
  117.8 0.1 constant_dynamic-update-slice_fusion.67
  117.9 0.1 constant_dynamic-update-slice_fusion.66
  118.0 0.1 constant_dynamic-update-slice_fusion.77
  118.1 0.1 constant_dynamic-update-slice_fusion.63
  118.2 0.7 copy-done.4
  118.9 0.1 constant_dynamic-update-slice_fusion.62
  119.0 0.1 constant_dynamic-update-slice_fusion.61
  119.1 0.1 constant_dynamic-update-slice_fusion.60
  119.2 0.1 constant_dynamic-update-slice_fusion.59
  119.3 0.1 constant_dynamic-update-slice_fusion.58
  119.4 0.8 copy-done.6
  (97 shorter events, 1.3 us)
Async XLA Ops:
  0.6 44.2 %copy-start.3 = (f32[19,4,16,128]{3,2,1,0:T(8,128)S(1)}, f32[19,4,16,128]{3,2,1,0:T(8,128)}, u32[]{:S(2)}) copy-start(f32[19,4,16,128]{3,2,1,0:T(8,128)} %param.4) | copy-start | bytes 1867780
  0.6 44.0 %copy-start.2 = (f32[19,4,16,128]{3,2,1,0:T(8,128)S(1)}, f32[19,4,16,128]{3,2,1,0:T(8,128)}, u32[]{:S(2)}) copy-start(f32[19,4,16,128]{3,2,1,0:T(8,128)} %param.3) | copy-start | bytes 1867780
  1.9 11.4 %collective-permute-start.3 = (f32[4,1,128]{2,1,0:T(1,128)S(1)}, f32[4,1,128]{2,1,0:T(1,128)S(1)}, u32[]{:S(2)}, u32[]{:S(2)}) collective-permute-start(f32[4,1,128]{2,1,0:T(1,128)S(1)} %get-tuple-element.108), channel_id=1, source_target_pairs={{2,0},{4,2},{6,4},{0,6},{3,1},{5,3},{7,5},{1,7},{10,8},{12,10},{14... | collective-permute-start | bytes 6152 | tf_op jit(solution)/shard_map/ppermute | solution.py:42
  2.8 10.5 %collective-permute-start.2 = (f32[4,1,128]{2,1,0:T(1,128)S(1)}, f32[4,1,128]{2,1,0:T(1,128)S(1)}, u32[]{:S(2)}, u32[]{:S(2)}) collective-permute-start(f32[4,1,128]{2,1,0:T(1,128)S(1)} %get-tuple-element.109), channel_id=1, source_target_pairs={{0,2},{2,4},{4,6},{6,0},{1,3},{3,5},{5,7},{7,1},{8,10},{10,12},{12... | collective-permute-start | bytes 6152 | tf_op jit(solution)/shard_map/ppermute | solution.py:40
  5.2 26.1 %collective-permute-start.1 = (f32[1,1,16,128]{3,2,1,0:T(8,128)S(1)}, f32[1,1,16,128]{3,2,1,0:T(8,128)S(1)}, u32[]{:S(2)}, u32[]{:S(2)}) collective-permute-start(f32[1,1,16,128]{3,2,1,0:T(8,128)S(1)} %get-tuple-element.114), channel_id=1, source_target_pairs={{8,0},{16,8},{24,16},{32,24},{40,32},{48,40},{56,48},{64,56},{72,6... | collective-permute-start | bytes 24584 | tf_op jit(solution)/shard_map/ppermute | solution.py:42
  11.2 8.1 %collective-permute-start = (f32[1,1,16,128]{3,2,1,0:T(8,128)S(1)}, f32[1,1,16,128]{3,2,1,0:T(8,128)S(1)}, u32[]{:S(2)}, u32[]{:S(2)}) collective-permute-start(f32[1,1,16,128]{3,2,1,0:T(8,128)S(1)} %get-tuple-element.115), channel_id=1, source_target_pairs={{0,8},{8,16},{16,24},{24,32},{32,40},{40,48},{48,56},{56,64},{64,7... | collective-permute-start | bytes 24584 | tf_op jit(solution)/shard_map/ppermute | solution.py:40
  13.4 29.9 %collective-permute-start.5 = (f32[4,18,1]{2,1,0:T(8,128)S(1)}, f32[4,18,1]{2,1,0:T(8,128)S(1)}, u32[]{:S(2)}, u32[]{:S(2)}) collective-permute-start(f32[4,18,1]{2,1,0:T(8,128)S(1)} %get-tuple-element.106), channel_id=1, source_target_pairs={{1,0},{0,1},{3,2},{2,3},{5,4},{4,5},{7,6},{6,7},{9,8},{8,9},{11,10... | collective-permute-start | bytes 872 | tf_op jit(solution)/shard_map/ppermute | solution.py:42
  17.9 25.3 %collective-permute-start.4 = (f32[4,18,1]{2,1,0:T(8,128)S(1)}, f32[4,18,1]{2,1,0:T(8,128)S(1)}, u32[]{:S(2)}, u32[]{:S(2)}) collective-permute-start(f32[4,18,1]{2,1,0:T(8,128)S(1)} %get-tuple-element.107), channel_id=1, source_target_pairs={{0,1},{1,0},{2,3},{3,2},{4,5},{5,4},{6,7},{7,6},{8,9},{9,8},{10,11... | collective-permute-start | bytes 872 | tf_op jit(solution)/shard_map/ppermute | solution.py:40
  45.4 20.5 %collective-permute-start.7 = (f32[10,1,16,128]{3,2,1,0:T(8,128)S(1)}, f32[10,1,16,128]{3,2,1,0:T(8,128)S(1)}, u32[]{:S(2)}, u32[]{:S(2)}) collective-permute-start(f32[10,1,16,128]{3,2,1,0:T(8,128)S(1)} %get-tuple-element.92), channel_id=1, source_target_pairs={{8,0},{16,8},{24,16},{32,24},{40,32},{48,40},{56,48},{64,56},{72,6... | collective-permute-start | bytes 245768 | tf_op jit(solution)/shard_map/ppermute | solution.py:42
  45.5 7.9 %collective-permute-start.6 = (f32[10,1,16,128]{3,2,1,0:T(8,128)S(1)}, f32[10,1,16,128]{3,2,1,0:T(8,128)S(1)}, u32[]{:S(2)}, u32[]{:S(2)}) collective-permute-start(f32[10,1,16,128]{3,2,1,0:T(8,128)S(1)} %get-tuple-element.93), channel_id=1, source_target_pairs={{0,8},{8,16},{16,24},{24,32},{32,40},{40,48},{48,56},{56,64},{64,7... | collective-permute-start | bytes 245768 | tf_op jit(solution)/shard_map/ppermute | solution.py:40
  78.9 5.0 %collective-permute-start.8 = (f32[38,6,1,128]{3,0,2,1:T(8,128)S(1)}, f32[38,6,1,128]{3,0,2,1:T(8,128)S(1)}, u32[]{:S(2)}, u32[]{:S(2)}) collective-permute-start(f32[38,6,1,128]{3,0,2,1:T(8,128)S(1)} %copy.288), channel_id=1, source_target_pairs={{0,2},{2,4},{4,6},{6,0},{1,3},{3,5},{5,7},{7,1},{8,10},{10,12},{12... | collective-permute-start | bytes 350216 | tf_op jit(solution)/shard_map/ppermute | solution.py:40
  79.6 6.3 %collective-permute-start.9 = (f32[38,6,1,128]{3,0,2,1:T(8,128)S(1)}, f32[38,6,1,128]{3,0,2,1:T(8,128)S(1)}, u32[]{:S(2)}, u32[]{:S(2)}) collective-permute-start(f32[38,6,1,128]{3,0,2,1:T(8,128)S(1)} %copy.290), channel_id=1, source_target_pairs={{2,0},{4,2},{6,4},{0,6},{3,1},{5,3},{7,5},{1,7},{10,8},{12,10},{14... | collective-permute-start | bytes 350216 | tf_op jit(solution)/shard_map/ppermute | solution.py:42
  92.8 9.1 %collective-permute-start.10 = (f32[38,6,18,1]{0,2,3,1:T(8,128)S(1)}, f32[38,6,18,1]{0,2,3,1:T(8,128)S(1)}, u32[]{:S(2)}, u32[]{:S(2)}) collective-permute-start(f32[38,6,18,1]{0,2,3,1:T(8,128)S(1)} %copy.294), channel_id=1, source_target_pairs={{0,1},{1,0},{2,3},{3,2},{4,5},{5,4},{6,7},{7,6},{8,9},{9,8},{10,11... | collective-permute-start | bytes 49256 | tf_op jit(solution)/shard_map/ppermute | solution.py:40
  100.4 8.3 %collective-permute-start.11 = (f32[38,6,18,1]{0,2,3,1:T(8,128)S(1)}, f32[38,6,18,1]{0,2,3,1:T(8,128)S(1)}, u32[]{:S(2)}, u32[]{:S(2)}) collective-permute-start(f32[38,6,18,1]{0,2,3,1:T(8,128)S(1)} %copy.296), channel_id=1, source_target_pairs={{1,0},{0,1},{3,2},{2,3},{5,4},{4,5},{7,6},{6,7},{9,8},{8,9},{11,10... | collective-permute-start | bytes 49256 | tf_op jit(solution)/shard_map/ppermute | solution.py:42
  112.4 1.8 %copy-start.1 = (f32[38,6,18,1]{3,2,1,0:T(8,128)S(1)}, f32[38,6,18,1]{3,2,1,0:T(8,128)}, u32[]{:S(2)}) copy-start(f32[38,6,18,1]{3,2,1,0:T(8,128)} %copy.297) | copy-start | bytes 49252
  114.2 1.8 %copy-start = (f32[38,6,18,1]{3,2,1,0:T(8,128)S(1)}, f32[38,6,18,1]{3,2,1,0:T(8,128)}, u32[]{:S(2)}) copy-start(f32[38,6,18,1]{3,2,1,0:T(8,128)} %copy.295) | copy-start | bytes 49252
  116.2 1.1 copy-start.5
  118.1 0.8 copy-start.4
  119.4 0.8 copy-start.6
where the time goes:
time: 121 us; the launch traced here: 120 us
  blocking collectives  48.6 us (40%)
  starting transfers between devices  24.3 us (20%)
  local copies, waits for them, and re-layouts  22.6 us (19%)
  waiting for transfers between devices  13.7 us (11%)
  other arithmetic  8.9 us (7%)
  between operations  2.11 us (2%)
    all_gather x2, blocking collectives, sliding(): lax.all_gather(above, 'gy', axis=1, tiled=True)  24.3 us
    all_gather x2, blocking collectives, sliding(): lax.all_gather(below, 'gy', axis=1, tiled=True)  24.3 us
    ppermute x6, starting transfers between devices, with_halo(): lax.ppermute(head, axis, [((i + 1) % count, i) for i in range(count)])  14.7 us
    ppermute x6, starting transfers between devices, with_halo(): lax.ppermute(tail, axis, [(i, (i + 1) % count) for i in range(count)])  9.57 us
    ppermute x6, waiting for transfers between devices, with_halo(): lax.ppermute(tail, axis, [(i, (i + 1) % count) for i in range(count)])  8.57 us
    unnamed x27, local copies, waits for them, and re-layouts  6.9 us
    slice x7, local copies, waits for them, and re-layouts, with_halo(): head = lax.slice_in_dim(cells, 0, width, axis=dim)  6.39 us
    ppermute x6, waiting for transfers between devices, with_halo(): lax.ppermute(head, axis, [((i + 1) % count, i) for i in range(count)])  5.11 us
  transfers between devices with their start and end apart: 12, of which 4 were waited for; matrix products, arithmetic and copies ran while one was open for 8% of the time, Pallas kernels for 0%

commit v1 on v0

--- a/solution.py
+++ b/solution.py
@@ -114,8 +114,16 @@
     extended = with_halo(edges, (("gx", 1),), 1)
     below = extended[:, 0]
     above = extended[:, 3]
+
+    def _take_plane(mat, group_axis):
+        arr_out = lax.axis_size(group_axis)
+        top = jnp.stack(arr_out * [mat])
+        state_now = lax.all_to_all(top, group_axis, 0, 0)
+        item_now = jnp.concatenate(state_now, axis=1)
+        return item_now
+
     whole_below, whole_above = (
-        lax.all_gather(below, "gy", axis=1, tiled=True),
+        _take_plane(below, "gy"),
         lax.all_gather(above, "gy", axis=1, tiled=True),
     )
     rows = below.shape[1]

time: 121 us -> 110 us (0.909)
  blocking collectives: 48.6 us -> 24.3 us
  starting transfers between devices: 24.3 us -> 34.5 us
  waiting for transfers between devices: 13.7 us -> 15.4 us
    all_gather x2 -> x0, blocking collectives: 24.3 us -> none  [sliding(): lax.all_gather(below, 'gy', axis=1, tiled=True)]
    all_to_all x0 -> x2, starting transfers between devices: none -> 9.01 us  [_take_plane(): state_now = lax.all_to_all(top, group_axis, 0, 0)]
    another operation x3 -> x5, local copies, waits for them, and re-layouts: 0.01 us -> 1.37 us  [the longest x2 1.37 us: _take_plane(): top = jnp.stack(arr_out * [mat])]
    ppermute x6, waiting for transfers between devices: 5.11 us -> 6.43 us  [with_halo(): lax.ppermute(head, axis, [((i + 1) % count, i) for i in range(count)])]
    unnamed x27 -> x25, local copies, waits for them, and re-layouts: 6.9 us -> 7.14 us
    ppermute x3 -> x2, local copies, waits for them, and re-layouts: 2.97 us -> 2.8 us  [with_halo(): lax.ppermute(tail, axis, [(i, (i + 1) % count) for i in range(count)])]
    unnamed x56 -> x60, other arithmetic: 3.92 us -> 3.97 us
  transfers between devices with their start and end apart: 12 -> 14, of which waited for: 4 -> 4; matrix products, arithmetic and copies ran while one was open for 8% -> 10% of each run, Pallas kernels for 0% -> 0%
where the time goes in v1:
time: 110 us; the launch traced here: 109 us
  starting transfers between devices  34.5 us (31%)
  blocking collectives  24.3 us (22%)
  local copies, waits for them, and re-layouts  23.6 us (21%)
  waiting for transfers between devices  15.4 us (14%)
  other arithmetic  8.94 us (8%)
  between operations  2.11 us (2%)
    all_gather x2, blocking collectives, sliding(): lax.all_gather(above, 'gy', axis=1, tiled=True)  24.3 us
    ppermute x6, starting transfers between devices, with_halo(): lax.ppermute(head, axis, [((i + 1) % count, i) for i in range(count)])  15.1 us
    ppermute x6, starting transfers between devices, with_halo(): lax.ppermute(tail, axis, [(i, (i + 1) % count) for i in range(count)])  10.3 us
    all_to_all x2, starting transfers between devices, _take_plane(): state_now = lax.all_to_all(top, group_axis, 0, 0)  9.01 us
    ppermute x6, waiting for transfers between devices, with_halo(): lax.ppermute(tail, axis, [(i, (i + 1) % count) for i in range(count)])  8.96 us
    unnamed x25, local copies, waits for them, and re-layouts  7.14 us
    ppermute x6, waiting for transfers between devices, with_halo(): lax.ppermute(head, axis, [((i + 1) % count, i) for i in range(count)])  6.43 us
    slice x7, local copies, waits for them, and re-layouts, with_halo(): head = lax.slice_in_dim(cells, 0, width, axis=dim)  6.24 us
  transfers between devices with their start and end apart: 14, of which 4 were waited for; matrix products, arithmetic and copies ran while one was open for 10% of the time, Pallas kernels for 0%

profile of v1, /device:TPU:6, one launch (start us, length us, event | category | flops | bytes accessed | tf_op | source)
XLA Modules:
  0.0 108.9 jit_solution(635646805045040462)
XLA Ops:
  0.7 1.2 %reduce_sum.19 = f32[4,16,128]{2,1,0:T(8,128)S(1)} reduce(f32[19,4,16,128]{3,2,1,0:T(8,128)} %param.4, f32[]{:T(128)} %constant.95.clone.1), dimensions={0}, to_apply=%region_1.2 | reduce | flops 147456 | bytes 655364 | tf_op jit(solution)/shard_map/reduce_sum | solution.py:162
  1.9 0.9 collective-permute-start.3
  2.8 2.4 %collective-permute-start.2 = (f32[4,1,128]{2,1,0:T(1,128)S(1)}, f32[4,1,128]{2,1,0:T(1,128)S(1)}, u32[]{:S(2)}, u32[]{:S(2)}) collective-permute-start(f32[4,1,128]{2,1,0:T(1,128)S(1)} %get-tuple-element.101), channel_id=1, source_target_pairs={{0,2},{2,4},{4,6},{6,0},{1,3},{3,5},{5,7},{7,1},{8,10},{10,12},{12... | collective-permute-start | bytes 6152 | tf_op jit(solution)/shard_map/ppermute | solution.py:40
  5.2 6.0 %collective-permute-start.1 = (f32[1,1,16,128]{3,2,1,0:T(8,128)S(1)}, f32[1,1,16,128]{3,2,1,0:T(8,128)S(1)}, u32[]{:S(2)}, u32[]{:S(2)}) collective-permute-start(f32[1,1,16,128]{3,2,1,0:T(8,128)S(1)} %get-tuple-element.106), channel_id=1, source_target_pairs={{8,0},{16,8},{24,16},{32,24},{40,32},{48,40},{56,48},{64,56},{72,6... | collective-permute-start | bytes 24584 | tf_op jit(solution)/shard_map/ppermute | solution.py:42
  12.0 0.1 pad.67.clone
  12.1 0.1 pad.60.clone
  12.1 1.1 %reduce_sum.18 = f32[4,16,128]{2,1,0:T(8,128)S(1)} reduce(f32[19,4,16,128]{3,2,1,0:T(8,128)} %param.3, f32[]{:T(128)} %constant.95.clone.1), dimensions={0}, to_apply=%region_0.0 | reduce | flops 147456 | bytes 655364 | tf_op jit(solution)/shard_map/reduce_sum | solution.py:68
  13.3 0.1 fusion.109
  13.4 4.5 %collective-permute-start.5 = (f32[4,18,1]{2,1,0:T(8,128)S(1)}, f32[4,18,1]{2,1,0:T(8,128)S(1)}, u32[]{:S(2)}, u32[]{:S(2)}) collective-permute-start(f32[4,18,1]{2,1,0:T(8,128)S(1)} %get-tuple-element.98), channel_id=1, source_target_pairs={{1,0},{0,1},{3,2},{2,3},{5,4},{4,5},{7,6},{6,7},{9,8},{8,9},{11,10... | collective-permute-start | bytes 872 | tf_op jit(solution)/shard_map/ppermute | solution.py:42
  17.9 1.4 %collective-permute-start.4 = (f32[4,18,1]{2,1,0:T(8,128)S(1)}, f32[4,18,1]{2,1,0:T(8,128)S(1)}, u32[]{:S(2)}, u32[]{:S(2)}) collective-permute-start(f32[4,18,1]{2,1,0:T(8,128)S(1)} %get-tuple-element.99), channel_id=1, source_target_pairs={{0,1},{1,0},{2,3},{3,2},{4,5},{5,4},{6,7},{7,6},{8,9},{9,8},{10,11... | collective-permute-start | bytes 872 | tf_op jit(solution)/shard_map/ppermute | solution.py:40
  19.4 0.6 stack.152
  20.0 4.5 %all-to-all-start = ((f32[4,1,16,128]{3,2,1,0:T(8,128)}), f32[4,1,16,128]{3,2,1,0:T(8,128)S(1)}, u32[]{:S(2)}, u32[]{:S(2)}) async-start(f32[4,1,16,128]{3,2,1,0:T(8,128)} %stack.152), calls=%async_computation | async-start | bytes 65536 | tf_op jit(solution)/shard_map/all_to_all | solution.py:121
  24.5 11.9 %all-gather = f32[1,1,64,128]{3,2,1,0:T(8,128)S(1)} all-gather(f32[1,1,16,128]{3,2,1,0:T(8,128)S(1)} %collective-permute-done.1), channel_id=2, replica_groups=mesh['gx'=32,'gy'=4,'gz'=2] {'gy'}, dimensions={2}, use_global_device_ids=true | all-gather | bytes 40960 | tf_op jit(solution)/shard_map/all_gather | solution.py:127
  36.5 1.4 %bitcast_subtract_fusion.16 = (f32[4,16,128]{2,1,0:T(8,128)S(1)}, f32[4,16,128]{2,1,0:T(8,128)S(1)}, f32[4,16,128]{2,1,0:T(8,128)S(1)}, f32[4,16,128]{2,1,0:T(8,...) fusion(f32[4,16,128]{2,1,0:T(8,128)S(1)} %reduce_sum.19, ...), kind=kLoop, calls=%fused_computation.191 | loop fusion | flops 2064384 | bytes 1512000 | tf_op jit(solution)/shard_map/sub | solution.py:103
  38.6 1.7 %collective-permute-start.7 = (f32[10,1,16,128]{3,2,0,1:T(8,128)S(1)}, f32[10,1,16,128]{3,2,0,1:T(8,128)S(1)}, u32[]{:S(2)}, u32[]{:S(2)}) collective-permute-start(f32[10,1,16,128]{3,2,0,1:T(8,128)S(1)} %get-tuple-element.84), channel_id=1, source_target_pairs={{8,0},{16,8},{24,16},{32,24},{40,32},{48,40},{56,48},{64,56},{72,6... | collective-permute-start | bytes 245768 | tf_op jit(solution)/shard_map/ppermute | solution.py:42
  40.4 0.8 copy.352
  41.7 6.4 %collective-permute-done.6 = f32[10,1,16,128]{3,2,0,1:T(8,128)S(1)} collective-permute-done((f32[10,1,16,128]{3,2,0,1:T(8,128)S(1)}, f32[10,1,16,128]{3,2,0,1:T(8,128)S(1)}, u32[]{:S(2)}, u32[]{:S(2)}) %collective-permute-start.6) | collective-permute-done | bytes 81952 | tf_op jit(solution)/shard_map/ppermute | solution.py:40
  48.1 0.7 stack.180
  48.9 4.5 %all-to-all-start.1 = ((f32[4,10,16,128]{3,2,1,0:T(8,128)}), f32[4,10,16,128]{3,2,1,0:T(8,128)S(1)}, u32[]{:S(2)}, u32[]{:S(2)}) async-start(f32[4,10,16,128]{3,2,1,0:T(8,128)} %stack.180), calls=%async_computation.1 | async-start | bytes 655360 | tf_op jit(solution)/shard_map/all_to_all | solution.py:121
  53.4 0.1 copy.247
  53.5 12.4 %all-gather.1 = f32[10,1,64,128]{3,1,0,2:T(1,128)S(1)} all-gather(f32[10,1,16,128]{3,1,0,2:T(1,128)S(1)} %copy.247), channel_id=3, replica_groups=mesh['gx'=32,'gy'=4,'gz'=2] {'gy'}, dimensions={2}, use_global_device_ids=true | all-gather | bytes 409600 | tf_op jit(solution)/shard_map/all_gather | solution.py:127
  65.9 0.1 maximum_bitcast_fusion.1
  66.2 0.1 maximum_bitcast_fusion.2
  66.3 0.2 fusion
  66.5 1.9 %collective-permute-start.8 = (f32[38,6,1,128]{3,0,2,1:T(8,128)S(1)}, f32[38,6,1,128]{3,0,2,1:T(8,128)S(1)}, u32[]{:S(2)}, u32[]{:S(2)}) collective-permute-start(f32[38,6,1,128]{3,0,2,1:T(8,128)S(1)} %copy.267), channel_id=1, source_target_pairs={{0,2},{2,4},{4,6},{6,0},{1,3},{3,5},{5,7},{7,1},{8,10},{10,12},{12... | collective-permute-start | bytes 350216 | tf_op jit(solution)/shard_map/ppermute | solution.py:40
  68.4 0.5 collective-permute-start.9
  68.8 2.6 %collective-permute-done.8 = f32[38,6,1,128]{3,0,2,1:T(8,128)S(1)} collective-permute-done((f32[38,6,1,128]{3,0,2,1:T(8,128)S(1)}, f32[38,6,1,128]{3,0,2,1:T(8,128)S(1)}, u32[]{:S(2)}, u32[]{:S(2)}) %collective-permute-start.8) | collective-permute-done | bytes 116768 | tf_op jit(solution)/shard_map/ppermute | solution.py:40
  71.4 0.1 copy.268
  71.6 3.2 %collective-permute-done.9 = f32[38,6,1,128]{3,0,2,1:T(8,128)S(1)} collective-permute-done((f32[38,6,1,128]{3,0,2,1:T(8,128)S(1)}, f32[38,6,1,128]{3,0,2,1:T(8,128)S(1)}, u32[]{:S(2)}, u32[]{:S(2)}) %collective-permute-start.9) | collective-permute-done | bytes 116768 | tf_op jit(solution)/shard_map/ppermute | solution.py:42
  74.7 0.1 copy.270
  74.8 0.4 pad_maximum_fusion
  75.3 3.2 %fusion.105 = (f32[38,6,18,1]{3,2,0,1:T(8,128)}, f32[38,6,18,1]{3,2,0,1:T(8,128)}) fusion(f32[38,6,18,128]{3,2,0,1:T(8,128)S(1)} %pad_maximum_fusion), kind=kLoop, calls=%fused_computation.400 | loop fusion | bytes 65664 | tf_op jit(solution)/shard_map/slice | solution.py:36
  78.5 2.9 %copy.273 = f32[38,6,18,1]{0,2,3,1:T(8,128)S(1)} copy(f32[38,6,18,1]{3,2,0,1:T(8,128)} %get-tuple-element.55) | data formatting | bytes 32832 | tf_op jit(solution)/shard_map/slice | solution.py:37
  81.4 4.6 %collective-permute-start.10 = (f32[38,6,18,1]{0,2,3,1:T(8,128)S(1)}, f32[38,6,18,1]{0,2,3,1:T(8,128)S(1)}, u32[]{:S(2)}, u32[]{:S(2)}) collective-permute-start(f32[38,6,18,1]{0,2,3,1:T(8,128)S(1)} %copy.273), channel_id=1, source_target_pairs={{0,1},{1,0},{2,3},{3,2},{4,5},{5,4},{6,7},{7,6},{8,9},{9,8},{10,11... | collective-permute-start | bytes 49256 | tf_op jit(solution)/shard_map/ppermute | solution.py:40
  86.0 2.9 %copy.275 = f32[38,6,18,1]{0,2,3,1:T(8,128)S(1)} copy(f32[38,6,18,1]{3,2,0,1:T(8,128)} %get-tuple-element.54) | data formatting | bytes 32832 | tf_op jit(solution)/shard_map/slice | solution.py:36
  88.9 1.5 %collective-permute-start.11 = (f32[38,6,18,1]{0,2,3,1:T(8,128)S(1)}, f32[38,6,18,1]{0,2,3,1:T(8,128)S(1)}, u32[]{:S(2)}, u32[]{:S(2)}) collective-permute-start(f32[38,6,18,1]{0,2,3,1:T(8,128)S(1)} %copy.275), channel_id=1, source_target_pairs={{1,0},{0,1},{3,2},{2,3},{5,4},{4,5},{7,6},{6,7},{9,8},{8,9},{11,10... | collective-permute-start | bytes 49256 | tf_op jit(solution)/shard_map/ppermute | solution.py:42
  90.4 2.7 %copy.274 = f32[38,6,18,1]{3,2,0,1:T(8,128)} copy(f32[38,6,18,1]{0,2,3,1:T(8,128)S(1)} %collective-permute-done.10) | data formatting | bytes 32832 | tf_op jit(solution)/shard_map/ppermute | solution.py:40
  93.1 0.9 constant_dynamic-update-slice_fusion.91
  94.0 3.3 %collective-permute-done.11 = f32[38,6,18,1]{0,2,3,1:T(8,128)S(1)} collective-permute-done((f32[38,6,18,1]{0,2,3,1:T(8,128)S(1)}, f32[38,6,18,1]{0,2,3,1:T(8,128)S(1)}, u32[]{:S(2)}, u32[]{:S(2)}) %collective-permute-start.11) | collective-permute-done | bytes 16448 | tf_op jit(solution)/shard_map/ppermute | solution.py:42
  97.2 2.7 %copy.276 = f32[38,6,18,1]{3,2,0,1:T(8,128)} copy(f32[38,6,18,1]{0,2,3,1:T(8,128)S(1)} %collective-permute-done.11) | data formatting | bytes 32832 | tf_op jit(solution)/shard_map/ppermute | solution.py:42
  100.0 0.9 constant_dynamic-update-slice_fusion.90
  100.9 1.7 %copy-done.1 = f32[38,6,18,1]{3,2,0,1:T(8,128)S(1)} copy-done((f32[38,6,18,1]{3,2,0,1:T(8,128)S(1)}, f32[38,6,18,1]{3,2,0,1:T(8,128)}, u32[]{:S(2)}) %copy-start.1) | copy-done | bytes 16440
  102.6 0.1 constant_dynamic-update-slice_fusion.86
  102.7 1.7 %copy-done = f32[38,6,18,1]{3,2,0,1:T(8,128)S(1)} copy-done((f32[38,6,18,1]{3,2,0,1:T(8,128)S(1)}, f32[38,6,18,1]{3,2,0,1:T(8,128)}, u32[]{:S(2)}) %copy-start) | copy-done | bytes 16440
  104.4 0.1 constant_dynamic-update-slice_fusion.85
  104.5 0.1 constant_dynamic-update-slice_fusion.82
  104.6 0.1 constant_dynamic-update-slice_fusion.81
  104.7 1.0 copy-done.4
  105.7 0.1 constant_dynamic-update-slice_fusion.80
  105.8 0.1 constant_dynamic-update-slice_fusion.79
  105.9 0.1 constant_dynamic-update-slice_fusion.72
  106.0 0.1 constant_dynamic-update-slice_fusion.71
  106.1 0.1 constant_dynamic-update-slice_fusion.78
  106.2 0.1 constant_dynamic-update-slice_fusion.67
  106.3 0.1 constant_dynamic-update-slice_fusion.66
  106.4 0.1 constant_dynamic-update-slice_fusion.77
  106.5 0.9 copy.280
  107.4 0.1 constant_dynamic-update-slice_fusion.63
  107.5 0.1 constant_dynamic-update-slice_fusion.62
  107.6 0.1 constant_dynamic-update-slice_fusion.61
  107.7 0.1 constant_dynamic-update-slice_fusion.60
  107.8 0.1 constant_dynamic-update-slice_fusion.59
  107.9 0.1 constant_dynamic-update-slice_fusion.58
  108.0 0.9 copy.279
  (102 shorter events, 1.3 us)
Async XLA Ops:
  0.6 37.3 %copy-start.3 = (f32[19,4,16,128]{3,2,1,0:T(8,128)S(1)}, f32[19,4,16,128]{3,2,1,0:T(8,128)}, u32[]{:S(2)}) copy-start(f32[19,4,16,128]{3,2,1,0:T(8,128)} %param.4) | copy-start | bytes 1867780
  0.6 37.3 %copy-start.2 = (f32[19,4,16,128]{3,2,1,0:T(8,128)S(1)}, f32[19,4,16,128]{3,2,1,0:T(8,128)}, u32[]{:S(2)}) copy-start(f32[19,4,16,128]{3,2,1,0:T(8,128)} %param.3) | copy-start | bytes 1867780
  1.9 11.4 %collective-permute-start.3 = (f32[4,1,128]{2,1,0:T(1,128)S(1)}, f32[4,1,128]{2,1,0:T(1,128)S(1)}, u32[]{:S(2)}, u32[]{:S(2)}) collective-permute-start(f32[4,1,128]{2,1,0:T(1,128)S(1)} %get-tuple-element.100), channel_id=1, source_target_pairs={{2,0},{4,2},{6,4},{0,6},{3,1},{5,3},{7,5},{1,7},{10,8},{12,10},{14... | collective-permute-start | bytes 6152 | tf_op jit(solution)/shard_map/ppermute | solution.py:42
  2.8 10.5 %collective-permute-start.2 = (f32[4,1,128]{2,1,0:T(1,128)S(1)}, f32[4,1,128]{2,1,0:T(1,128)S(1)}, u32[]{:S(2)}, u32[]{:S(2)}) collective-permute-start(f32[4,1,128]{2,1,0:T(1,128)S(1)} %get-tuple-element.101), channel_id=1, source_target_pairs={{0,2},{2,4},{4,6},{6,0},{1,3},{3,5},{5,7},{7,1},{8,10},{10,12},{12... | collective-permute-start | bytes 6152 | tf_op jit(solution)/shard_map/ppermute | solution.py:40
  5.2 19.3 %collective-permute-start.1 = (f32[1,1,16,128]{3,2,1,0:T(8,128)S(1)}, f32[1,1,16,128]{3,2,1,0:T(8,128)S(1)}, u32[]{:S(2)}, u32[]{:S(2)}) collective-permute-start(f32[1,1,16,128]{3,2,1,0:T(8,128)S(1)} %get-tuple-element.106), channel_id=1, source_target_pairs={{8,0},{16,8},{24,16},{32,24},{40,32},{48,40},{56,48},{64,56},{72,6... | collective-permute-start | bytes 24584 | tf_op jit(solution)/shard_map/ppermute | solution.py:42
  11.2 8.1 %collective-permute-start = (f32[1,1,16,128]{3,2,1,0:T(8,128)S(1)}, f32[1,1,16,128]{3,2,1,0:T(8,128)S(1)}, u32[]{:S(2)}, u32[]{:S(2)}) collective-permute-start(f32[1,1,16,128]{3,2,1,0:T(8,128)S(1)} %get-tuple-element.107), channel_id=1, source_target_pairs={{0,8},{8,16},{16,24},{24,32},{32,40},{40,48},{48,56},{56,64},{64,7... | collective-permute-start | bytes 24584 | tf_op jit(solution)/shard_map/ppermute | solution.py:40
  13.4 23.1 %collective-permute-start.5 = (f32[4,18,1]{2,1,0:T(8,128)S(1)}, f32[4,18,1]{2,1,0:T(8,128)S(1)}, u32[]{:S(2)}, u32[]{:S(2)}) collective-permute-start(f32[4,18,1]{2,1,0:T(8,128)S(1)} %get-tuple-element.98), channel_id=1, source_target_pairs={{1,0},{0,1},{3,2},{2,3},{5,4},{4,5},{7,6},{6,7},{9,8},{8,9},{11,10... | collective-permute-start | bytes 872 | tf_op jit(solution)/shard_map/ppermute | solution.py:42
  17.9 18.6 %collective-permute-start.4 = (f32[4,18,1]{2,1,0:T(8,128)S(1)}, f32[4,18,1]{2,1,0:T(8,128)S(1)}, u32[]{:S(2)}, u32[]{:S(2)}) collective-permute-start(f32[4,18,1]{2,1,0:T(8,128)S(1)} %get-tuple-element.99), channel_id=1, source_target_pairs={{0,1},{1,0},{2,3},{3,2},{4,5},{5,4},{6,7},{7,6},{8,9},{9,8},{10,11... | collective-permute-start | bytes 872 | tf_op jit(solution)/shard_map/ppermute | solution.py:40
  20.0 16.4 %all-to-all-start = ((f32[4,1,16,128]{3,2,1,0:T(8,128)}), f32[4,1,16,128]{3,2,1,0:T(8,128)S(1)}, u32[]{:S(2)}, u32[]{:S(2)}) async-start(f32[4,1,16,128]{3,2,1,0:T(8,128)} %stack.152), calls=%async_computation | async-start | bytes 65536 | tf_op jit(solution)/shard_map/all_to_all | solution.py:121
  38.6 14.7 %collective-permute-start.7 = (f32[10,1,16,128]{3,2,0,1:T(8,128)S(1)}, f32[10,1,16,128]{3,2,0,1:T(8,128)S(1)}, u32[]{:S(2)}, u32[]{:S(2)}) collective-permute-start(f32[10,1,16,128]{3,2,0,1:T(8,128)S(1)} %get-tuple-element.84), channel_id=1, source_target_pairs={{8,0},{16,8},{24,16},{32,24},{40,32},{48,40},{56,48},{64,56},{72,6... | collective-permute-start | bytes 245768 | tf_op jit(solution)/shard_map/ppermute | solution.py:42
  40.3 7.8 %collective-permute-start.6 = (f32[10,1,16,128]{3,2,0,1:T(8,128)S(1)}, f32[10,1,16,128]{3,2,0,1:T(8,128)S(1)}, u32[]{:S(2)}, u32[]{:S(2)}) collective-permute-start(f32[10,1,16,128]{3,2,0,1:T(8,128)S(1)} %get-tuple-element.85), channel_id=1, source_target_pairs={{0,8},{8,16},{16,24},{24,32},{32,40},{40,48},{48,56},{56,64},{64,7... | collective-permute-start | bytes 245768 | tf_op jit(solution)/shard_map/ppermute | solution.py:40
  48.9 17.2 %all-to-all-start.1 = ((f32[4,10,16,128]{3,2,1,0:T(8,128)}), f32[4,10,16,128]{3,2,1,0:T(8,128)S(1)}, u32[]{:S(2)}, u32[]{:S(2)}) async-start(f32[4,10,16,128]{3,2,1,0:T(8,128)} %stack.180), calls=%async_computation.1 | async-start | bytes 655360 | tf_op jit(solution)/shard_map/all_to_all | solution.py:121
  66.5 5.0 %collective-permute-start.8 = (f32[38,6,1,128]{3,0,2,1:T(8,128)S(1)}, f32[38,6,1,128]{3,0,2,1:T(8,128)S(1)}, u32[]{:S(2)}, u32[]{:S(2)}) collective-permute-start(f32[38,6,1,128]{3,0,2,1:T(8,128)S(1)} %copy.267), channel_id=1, source_target_pairs={{0,2},{2,4},{4,6},{6,0},{1,3},{3,5},{5,7},{7,1},{8,10},{10,12},{12... | collective-permute-start | bytes 350216 | tf_op jit(solution)/shard_map/ppermute | solution.py:40
  68.4 6.3 %collective-permute-start.9 = (f32[38,6,1,128]{3,0,2,1:T(8,128)S(1)}, f32[38,6,1,128]{3,0,2,1:T(8,128)S(1)}, u32[]{:S(2)}, u32[]{:S(2)}) collective-permute-start(f32[38,6,1,128]{3,0,2,1:T(8,128)S(1)} %copy.269), channel_id=1, source_target_pairs={{2,0},{4,2},{6,4},{0,6},{3,1},{5,3},{7,5},{1,7},{10,8},{12,10},{14... | collective-permute-start | bytes 350216 | tf_op jit(solution)/shard_map/ppermute | solution.py:42
  81.4 9.0 %collective-permute-start.10 = (f32[38,6,18,1]{0,2,3,1:T(8,128)S(1)}, f32[38,6,18,1]{0,2,3,1:T(8,128)S(1)}, u32[]{:S(2)}, u32[]{:S(2)}) collective-permute-start(f32[38,6,18,1]{0,2,3,1:T(8,128)S(1)} %copy.273), channel_id=1, source_target_pairs={{0,1},{1,0},{2,3},{3,2},{4,5},{5,4},{6,7},{7,6},{8,9},{9,8},{10,11... | collective-permute-start | bytes 49256 | tf_op jit(solution)/shard_map/ppermute | solution.py:40
  88.9 8.3 %collective-permute-start.11 = (f32[38,6,18,1]{0,2,3,1:T(8,128)S(1)}, f32[38,6,18,1]{0,2,3,1:T(8,128)S(1)}, u32[]{:S(2)}, u32[]{:S(2)}) collective-permute-start(f32[38,6,18,1]{0,2,3,1:T(8,128)S(1)} %copy.275), channel_id=1, source_target_pairs={{1,0},{0,1},{3,2},{2,3},{5,4},{4,5},{7,6},{6,7},{9,8},{8,9},{11,10... | collective-permute-start | bytes 49256 | tf_op jit(solution)/shard_map/ppermute | solution.py:42
  100.8 1.8 %copy-start.1 = (f32[38,6,18,1]{3,2,0,1:T(8,128)S(1)}, f32[38,6,18,1]{3,2,0,1:T(8,128)}, u32[]{:S(2)}) copy-start(f32[38,6,18,1]{3,2,0,1:T(8,128)} %copy.276) | copy-start | bytes 49252
  102.6 1.8 %copy-start = (f32[38,6,18,1]{3,2,0,1:T(8,128)S(1)}, f32[38,6,18,1]{3,2,0,1:T(8,128)}, u32[]{:S(2)}) copy-start(f32[38,6,18,1]{3,2,0,1:T(8,128)} %copy.274) | copy-start | bytes 49252
  104.6 1.1 copy-start.4
